TPU v7x, 128 devices: a whole 4x4x4 slice. The times are simulated.
128 devices in a mesh: ctx: 8 (over x, y_hi), head: 16 (over y_lo, z, core).
Axes of the slice: x: 4, y: 4 (y_hi: 2, y_lo: 2; y = y_hi * 2 + y_lo), z: 4, core: 2. Of those that a mesh axis runs over, the one named last changes fastest.
Arguments:
- hidden_in: bfloat16 [8192, 5376], P(('ctx', 'head')), may hold values from -6 to 6
- pre_gain: float32 [5376], replicated, may hold values from 0.1 to 1.9
- w_query: bfloat16 [5376, 4096], P('ctx', 'head'), may hold values from -0.054554473 to 0.054554473, as said below
- w_key: bfloat16 [5376, 2048], P('ctx', 'head'), may hold values from -0.054554473 to 0.054554473, as said below
- value_weight: bfloat16 [5376, 2048], P('ctx', 'head'), may hold values from -0.078125 to 0.078125
- query_gain: float32 [128], replicated, may hold values from 0.6 to 7, as said below
- key_norm_gain: float32 [128], replicated, may hold values from 0.6 to 7, as said below
- w_output: bfloat16 [4096, 5376], P(('head', 'ctx')), may hold values from -0.09375 to 0.09375
- post_gain: float32 [5376], replicated, may hold values from 0.1 to 1.9
Outputs:
- layer_out: bfloat16 [8192, 5376], P(('ctx', 'head'))
Inputs may be any that keep to these rules, and one draw needn't show every extreme that they name: `w_query`: entries are normal draws clipped to 4 standard deviations, scaled by 5376 ** -0.5. `w_key`: entries are normal draws clipped to 4 standard deviations, scaled by 5376 ** -0.5. `query_gain`: positive gains. `key_norm_gain`: positive gains.
All inputs are finite; a program needn't handle non-finite values.
Results may differ from a plain program's by a relative error of at most 0.015.
The roundings to bfloat16 on the way count: a program that leaves them out, or rounds other values in their place, can miss the bound.
Values may be sent and summed in bfloat16 or wider, within the bound.
No kernel may reach another device: no remote copies, remote signals or barrier semaphores. Data moves between devices by JAX's collectives and lax.ppermute only.
A program may use at most 64 MiB of HBM per device.

v0:
```python
import jax
import jax.numpy as jnp
from jax import lax
from jax.sharding import PartitionSpec as P

HEAD_SIZE = 128
WINDOW_SPAN = 1024
norm_eps = 1e-06
query_scale = 168.0 ** (-0.5)
rope_base = 10000.0
mask_value = -1e30


def passed_along(shard, axis, by):
    count = lax.axis_size(axis)
    pairs = [(i, i + by) for i in range(count) if 0 <= i + by < count]
    return lax.ppermute(shard, axis, pairs)


def root_mean_scale(values, scaling):
    mean_sq = jnp.mean(values * values, axis=-1, keepdims=True)
    return values * lax.rsqrt(mean_sq + norm_eps) * scaling


def apply_rotary(values, token_places):
    full_width = values.shape[-1]
    half_width = full_width // 2
    frequency = rope_base ** (-jnp.arange(half_width, dtype=jnp.float32) * 2.0 / full_width)
    angles = token_places.astype(jnp.float32)[:, None] * frequency[None, :]
    cosine = jnp.cos(angles)[:, None, :]
    sine_part = jnp.sin(angles)[:, None, :]
    lower_half = values[..., :half_width]
    upper_half = values[..., half_width:]
    return jnp.concatenate(
        [
            lower_half * cosine - upper_half * sine_part,
            upper_half * cosine + lower_half * sine_part,
        ],
        axis=-1,
    )


def body(
    hidden_in,
    pre_gain,
    w_query,
    w_key,
    value_weight,
    query_gain,
    key_norm_gain,
    w_output,
    post_gain,
):
    own_rows = hidden_in.astype(jnp.float32)
    raw_rows = lax.all_gather(hidden_in, "head", axis=0, tiled=True)
    normed = root_mean_scale(raw_rows.astype(jnp.float32), pre_gain).astype(jnp.bfloat16)
    tok_count = normed.shape[0]

    def add_rows(weight_piece):
        return jnp.dot(normed, weight_piece, preferred_element_type=jnp.float32)

    query_raw = add_rows(lax.all_gather(w_query, "ctx", axis=0, tiled=True))
    key_unnormed = add_rows(lax.all_gather(w_key, "ctx", axis=0, tiled=True))
    value_unnormed = add_rows(lax.all_gather(value_weight, "ctx", axis=0, tiled=True))
    local_heads = w_query.shape[1] // HEAD_SIZE
    local_groups = w_key.shape[1] // HEAD_SIZE
    heads_per_group = local_heads // local_groups
    ctx_index = lax.axis_index("ctx")
    token_places = ctx_index * tok_count + jnp.arange(tok_count, dtype=jnp.int32)
    query_matrix = (
        apply_rotary(
            root_mean_scale(query_raw.reshape(tok_count, local_heads, HEAD_SIZE), query_gain),
            token_places,
        )
        * query_scale
    ).astype(jnp.bfloat16)
    projected_keys = apply_rotary(
        root_mean_scale(key_unnormed.reshape(tok_count, local_groups, HEAD_SIZE), key_norm_gain),
        token_places,
    ).astype(jnp.bfloat16)
    projected_values = value_unnormed.astype(jnp.bfloat16)
    key_value = jnp.stack(
        [projected_keys.reshape(tok_count, local_groups * HEAD_SIZE), projected_values]
    )
    pieces = [passed_along(key_value, "ctx", 1)]
    extended = jnp.concatenate(pieces + [key_value], axis=1)
    band_keys = extended[0].reshape(-1, local_groups, HEAD_SIZE)
    band_values = extended[1].reshape(-1, local_groups, HEAD_SIZE)
    block_rows = min(512, tok_count)
    grouped_queries = query_matrix.reshape(tok_count, local_groups, heads_per_group, HEAD_SIZE)
    outputs = []
    for block_index in range(tok_count // block_rows):
        first_row = block_index * block_rows
        query_block = grouped_queries[first_row : first_row + block_rows]
        key_block = band_keys[first_row : first_row + block_rows + WINDOW_SPAN]
        value_block = band_values[first_row : first_row + block_rows + WINDOW_SPAN]
        scores = jnp.einsum(
            "qjgd,kjd->jgqk", query_block, key_block, preferred_element_type=jnp.float32
        )
        query_spots = token_places[first_row : first_row + block_rows]
        key_spots = (
            ctx_index * tok_count
            - WINDOW_SPAN
            + first_row
            + jnp.arange(block_rows + WINDOW_SPAN, dtype=jnp.int32)
        )
        allowed = (
            (key_spots[None, :] <= query_spots[:, None])
            & (key_spots[None, :] > query_spots[:, None] - WINDOW_SPAN)
            & (key_spots[None, :] >= 0)
        )
        scores = jnp.where(allowed, scores, mask_value)
        row_max = jnp.max(scores, axis=-1, keepdims=True)
        weights = jnp.exp(scores - row_max)
        row_sum = jnp.sum(weights, axis=-1, keepdims=True)
        probabilities = (weights / row_sum).astype(jnp.bfloat16)
        mixed = jnp.einsum(
            "jgqk,kjd->qjgd", probabilities, value_block, preferred_element_type=jnp.float32
        )
        outputs.append(mixed.astype(jnp.bfloat16).reshape(block_rows, local_heads * HEAD_SIZE))
    attended = jnp.concatenate(outputs, axis=0)
    out_weight = lax.all_gather(w_output, "ctx", axis=0, tiled=True)
    partial_value = jnp.dot(attended, out_weight, preferred_element_type=jnp.float32).astype(
        jnp.bfloat16
    )
    summed = lax.psum_scatter(
        lax.optimization_barrier(partial_value).astype(jnp.float32).astype(jnp.bfloat16),
        "head",
        scatter_dimension=0,
        tiled=True,
    ).astype(jnp.float32)
    result = own_rows + root_mean_scale(summed, post_gain)
    return result.astype(jnp.bfloat16)


def solution(mesh):
    return jax.shard_map(
        body,
        mesh=mesh,
        in_specs=(
            P(("ctx", "head"), None),
            P(),
            P("ctx", "head"),
            P("ctx", "head"),
            P("ctx", "head"),
            P(),
            P(),
            P(("head", "ctx"), None),
            P(),
        ),
        out_specs=P(("ctx", "head"), None),
        check_vma=False,
    )
```

profile of v0, /device:TPU:0, one launch (start us, length us, event | category | flops | bytes accessed | tf_op | source)
XLA Modules:
  0.0 400.9 jit_solution(7037838070945432475)
XLA Ops:
  6.5 0.0 all-gather.6.cloned.1.call-start
  6.5 0.7 all-gather.6.cloned.1.call-update
  7.3 0.0 all-gather.8.cloned.1.call-start
  7.3 0.7 all-gather.8.cloned.1.call-update
  8.0 0.0 all-gather.10.cloned.1.call-start
  8.1 0.7 all-gather.10.cloned.1.call-update
  8.7 0.0 all-gather.12.cloned.1.call-start
  8.8 0.5 all-gather.12.cloned.1.call-update
  9.3 0.0 all-gather.14.cloned.1.call-start
  9.4 0.5 all-gather.14.cloned.1.call-update
  9.9 0.0 reduce-scatter.2.cloned.1.call-start
  10.1 3.0 multiply_cosine_fusion
  13.1 0.0 copy-start.6
  13.1 1.8 and_and_fusion.1
  15.0 1.9 and_and_fusion
  16.8 59.2 %all-gather.6.cloned.1.call-done = bf16[1024,5376]{1,0:T(8,128)(2,1)} async-done(((bf16[64,5376]{1,0:T(8,128)(2,1)}), bf16[1024,5376]{1,0:T(8,128)(2,1)}) %all-gather.6.cloned.1.call-update) | async-done | bytes 11010064 | tf_op jit(solution)/shard_map/all_gather | solution.py:55
  76.0 0.0 copy-start
  76.0 6.5 %fusion = f32[1024]{0:T(1024)S(1)} fusion(bf16[1024,5376]{1,0:T(8,128)(2,1)} %all-gather.6.cloned.1.call-done), kind=kLoop, calls=%fused_computation.2 | loop fusion | flops 16514048 | bytes 11014144 | tf_op jit(solution)/shard_map/reduce_sum | solution.py:21
  82.5 0.0 copy-done.6
  82.5 0.8 copy-done
  83.3 6.0 %fusion.2 = bf16[1024,5376]{1,0:T(8,128)(2,1)} fusion(bf16[1024,5376]{1,0:T(8,128)(2,1)S(1)} %copy-done, f32[5376]{0:T(1024)S(1)} %copy-done.6, f32[1024]{0:T(1024)S(1)} %add_rsqrt_fusion.2), kind=kLoop, calls=%fused_computation.4 | loop fusion | flops 22020096 | bytes 22045696 | tf_op jit(solution)/shard_map/convert_element_type | solution.py:56
  89.2 0.0 copy-start.8
  89.2 39.5 %all-gather.8.cloned.1.call-done = bf16[5376,128]{1,0:T(8,128)(2,1)} async-done(((bf16[672,128]{1,0:T(8,128)(2,1)}), bf16[5376,128]{1,0:T(8,128)(2,1)}) %all-gather.8.cloned.1.call-update) | async-done | bytes 1376272 | tf_op jit(solution)/shard_map/all_gather | solution.py:63
  128.7 8.2 %multiply_reduce_fusion.1 = (f32[1024]{0:T(1024)S(1)}, f32[1024,128]{0,1:T(8,128)S(1)}) fusion(bf16[1024,5376]{1,0:T(8,128)(2,1)} %fusion.2, bf16[5376,128]{1,0:T(8,128)(2,1)} %all-gather.8.cloned.1.call-done), kind=kOutput, calls=%fused_computation.46 | convolution fusion | flops 1409547264 | bytes 12914688 | tf_op jit(solution)/shard_map/dot_general | solution.py:60
  137.0 0.0 copy-done.8
  137.0 0.1 multiply_bitcast_fusion
  137.1 1.2 fusion.39
  138.2 41.1 %all-gather.10.cloned.1.call-done = bf16[5376,128]{1,0:T(8,128)(2,1)} async-done(((bf16[672,128]{1,0:T(8,128)(2,1)}), bf16[5376,128]{1,0:T(8,128)(2,1)}) %all-gather.10.cloned.1.call-update) | async-done | bytes 1376272 | tf_op jit(solution)/shard_map/all_gather | solution.py:64
  179.3 8.2 %fusion.21 = bf16[1,1024,128]{1,2,0:T(8,128)(2,1)S(1)} fusion(bf16[1024,5376]{1,0:T(8,128)(2,1)} %fusion.2, bf16[5376,128]{1,0:T(8,128)(2,1)} %all-gather.10.cloned.1.call-done), kind=kOutput, calls=%fused_computation.31 | convolution fusion | flops 1409417216 | bytes 12648448 | tf_op jit(solution)/shard_map/dot_general | solution.py:60
  187.6 0.0 copy-start.9
  187.6 0.0 copy-start.4
  187.6 0.0 copy-start.5
  187.6 3.4 collective-permute-start
  191.0 52.1 %all-gather.12.cloned.1.call-done = bf16[5376,256]{1,0:T(8,128)(2,1)} async-done(((bf16[672,256]{1,0:T(8,128)(2,1)}), bf16[5376,256]{1,0:T(8,128)(2,1)}) %all-gather.12.cloned.1.call-update) | async-done | bytes 2752528 | tf_op jit(solution)/shard_map/all_gather | solution.py:62
  243.1 9.0 %multiply_reduce_fusion = (f32[1024,2]{0,1:T(2,128)S(1)}, f32[1024,256]{0,1:T(8,128)}) fusion(bf16[1024,5376]{1,0:T(8,128)(2,1)} %fusion.2, bf16[5376,256]{1,0:T(8,128)(2,1)} %all-gather.12.cloned.1.call-done), kind=kOutput, calls=%fused_computation.38 | convolution fusion | flops 2819094528 | bytes 14819328 | tf_op jit(solution)/shard_map/dot_general | solution.py:60
  252.1 1.6 copy.11
  253.7 0.0 copy-start.1
  253.7 0.0 copy-done.9
  253.7 0.3 multiply_multiply_fusion
  254.1 0.0 copy-done.4
  254.1 0.0 copy-done.5
  254.1 0.5 multiply_subtract_fusion
  254.6 0.0 copy-start.2
  254.6 0.3 fusion.22
  255.0 0.0 collective-permute-done
  255.0 1.1 maximum_maximum_fusion
  256.1 0.0 copy-done.1
  256.1 1.3 fusion.3
  257.4 0.0 copy-done.2
  257.4 1.3 fusion.4
  258.7 1.2 fusion.5
  260.0 1.2 fusion.6
  261.2 2.0 fusion.15
  263.2 2.2 fusion.18
  265.4 38.4 %all-gather.14.cloned.1.call-done = bf16[256,5376]{1,0:T(8,128)(2,1)} async-done(((bf16[32,5376]{1,0:T(8,128)(2,1)}), bf16[256,5376]{1,0:T(8,128)(2,1)}) %all-gather.14.cloned.1.call-update) | async-done | bytes 2752528 | tf_op jit(solution)/shard_map/all_gather | solution.py:122
  303.9 7.6 %convolution_convert_fusion = bf16[1024,5376]{1,0:T(8,128)(2,1)} fusion(bf16[256,5376]{1,0:T(8,128)(2,1)} %all-gather.14.cloned.1.call-done, bf16[512,256]{0,1:T(8,128)(2,1)S(1)} %bitcast.95, bf16[512,256]{0,1:T(8,128)(2,1)S(1)} %bitcast.94), kind=kOutput, calls=%fused_computation.5 | convolution fusion | flops 2825125888 | bytes 14286848 | tf_op jit(solution)/shard_map/dot_general | solution.py:123
  311.5 0.0 copy-start.3
  311.5 0.0 copy-start.7
  311.5 0.0 reduce-scatter.2.cloned.1.call-update
  311.5 78.9 %reduce-scatter.2.cloned.1.call-done = bf16[64,5376]{1,0:T(8,128)(2,1)} async-done(((bf16[1024,5376]{1,0:T(8,128)(2,1)}), bf16[64,5376]{1,0:T(8,128)(2,1)}) %reduce-scatter.2.cloned.1.call-update) | async-done | bytes 688144 | tf_op jit(solution)/shard_map/reduce_scatter | solution.py:126
  390.4 1.3 fusion.11
  391.8 0.0 copy-done.3
  391.8 0.0 copy-done.7
  391.8 2.3 fusion.14
  (12 shorter events, 0.1 us)
Async XLA Ops:
  6.5 69.5 %all-gather.6.cloned.1.call-start = ((), (), s32[]{:S(2)}) async-start(), calls=%async_computation.1 | async-start | bytes 11698176 | tf_op jit(solution)/shard_map/all_gather | solution.py:55
  7.3 121.5 %all-gather.8.cloned.1.call-start = ((), (), s32[]{:S(2)}) async-start(), calls=%async_computation.2 | async-start | bytes 1548288 | tf_op jit(solution)/shard_map/all_gather | solution.py:63
  8.0 171.3 %all-gather.10.cloned.1.call-start = ((), (), s32[]{:S(2)}) async-start(), calls=%async_computation.3 | async-start | bytes 1548288 | tf_op jit(solution)/shard_map/all_gather | solution.py:64
  8.7 234.4 %all-gather.12.cloned.1.call-start = ((), (), s32[]{:S(2)}) async-start(), calls=%async_computation.4 | async-start | bytes 3096576 | tf_op jit(solution)/shard_map/all_gather | solution.py:62
  9.3 294.5 %all-gather.14.cloned.1.call-start = ((), (), s32[]{:S(2)}) async-start(), calls=%async_computation.5 | async-start | bytes 3096576 | tf_op jit(solution)/shard_map/all_gather | solution.py:122
  9.9 380.5 %reduce-scatter.2.cloned.1.call-start = ((), (), s32[]{:S(2)}) async-start(), calls=%async_computation.6 | async-start | bytes 11698176 | tf_op jit(solution)/shard_map/reduce_scatter | solution.py:126
  13.1 69.4 %copy-start.6 = (f32[5376]{0:T(1024)S(1)}, f32[5376]{0:T(1024)}, u32[]{:S(2)}) copy-start(f32[5376]{0:T(1024)} %param.10) | copy-start | bytes 64516
  76.0 7.3 %copy-start = (bf16[1024,5376]{1,0:T(8,128)(2,1)S(1)}, bf16[1024,5376]{1,0:T(8,128)(2,1)}, u32[]{:S(2)}) copy-start(bf16[1024,5376]{1,0:T(8,128)(2,1)} %all-gather.6.cloned.1.call-done) | copy-start | bytes 33030148
  89.2 47.7 %copy-start.8 = (f32[128]{0:T(128)S(1)}, f32[128]{0:T(128)}, u32[]{:S(2)}) copy-start(f32[128]{0:T(128)} %param.15) | copy-start | bytes 1540
  187.6 66.1 %copy-start.9 = (f32[128]{0:T(128)S(1)}, f32[128]{0:T(128)}, u32[]{:S(2)}) copy-start(f32[128]{0:T(128)} %param.14) | copy-start | bytes 1540
  187.6 66.5 %copy-start.4 = (f32[1024,64]{1,0:T(8,128)S(1)}, f32[1024,64]{1,0:T(8,128)}, u32[]{:S(2)}) copy-start(f32[1024,64]{1,0:T(8,128)} %get-tuple-element.9) | copy-start | bytes 786436
  187.6 66.5 %copy-start.5 = (f32[1024,64]{1,0:T(8,128)S(1)}, f32[1024,64]{1,0:T(8,128)}, u32[]{:S(2)}) copy-start(f32[1024,64]{1,0:T(8,128)} %get-tuple-element.10) | copy-start | bytes 786436
  187.6 67.4 %collective-permute-start = (bf16[2,1024,128]{1,2,0:T(8,128)(2,1)S(1)}, bf16[2,1024,128]{1,2,0:T(8,128)(2,1)}, u32[]{:S(2)}, u32[]{:S(2)}) collective-permute-start(bf16[2,1024,128]{1,2,0:T(8,128)(2,1)S(1)} %pad_maximum_fusion), channel_id=1, source_target_pairs={{0,16},{16,32},{32,48},{48,64},{64,80},{80,96},{96,112},{1,17},{17... | collective-permute-start | bytes 1572872 | tf_op jit(solution)/shard_map/ppermute | solution.py:17
  253.7 2.4 copy-start.1
  254.6 2.8 copy-start.2
  311.5 80.3 %copy-start.3 = (bf16[64,5376]{1,0:T(8,128)(2,1)S(1)}, bf16[64,5376]{1,0:T(8,128)(2,1)}, u32[]{:S(2)}) copy-start(bf16[64,5376]{1,0:T(8,128)(2,1)} %param.9) | copy-start | bytes 2064388
  311.5 80.3 %copy-start.7 = (f32[5376]{0:T(1024)S(1)}, f32[5376]{0:T(1024)}, u32[]{:S(2)}) copy-start(f32[5376]{0:T(1024)} %param.17) | copy-start | bytes 64516
Sparse Core Ops, SparseCore 0:
  9.0 66.9 all-gather.5
  78.3 50.3 all-gather.7
  131.0 48.2 all-gather.9
  181.5 61.6 all-gather.11
  245.3 58.5 all-gather.13
  311.7 78.7 reduce-scatter.1
where the time goes:
time: 401 us
  waiting for transfers between devices  312 us (78%)
  matrix products  39.9 us (10%)
  other arithmetic  28.9 us (7%)
  between operations  13.8 us (3%)
    reduce_scatter x1, waiting for transfers between devices, body(): lax.psum_scatter(lax.optimization_barrier(partial_value).astype(jnp.float...  78.9 us
    all_gather x1, waiting for transfers between devices, body(): raw_rows = lax.all_gather(hidden_in, 'head', axis=0, tiled=True)  59.2 us
    all_gather x1, waiting for transfers between devices, body(): query_raw = add_rows(lax.all_gather(w_query, 'ctx', axis=0, tiled=True))  52.1 us
    all_gather x1, waiting for transfers between devices, body(): lax.all_gather(value_weight, 'ctx', axis=0, tiled=True)  41.1 us
    all_gather x1, waiting for transfers between devices, body(): key_unnormed = add_rows(lax.all_gather(w_key, 'ctx', axis=0, tiled=True))  39.5 us
    all_gather x1, waiting for transfers between devices, body(): out_weight = lax.all_gather(w_output, 'ctx', axis=0, tiled=True)  38.4 us
    dot_general x3, matrix products, add_rows(): return jnp.dot(normed, weight_piece, preferred_element_type=jnp.float32)  25.4 us
  transfers between devices with their start and end apart: 7, of which 6 were waited for; matrix products, arithmetic and copies ran while one was open for 15% of the time, Pallas kernels for 0%

commit v1 on v0

--- a/solution.py
+++ b/solution.py
@@ -51,6 +51,14 @@
     w_output,
     post_gain,
 ):
+
+    def stops_all_get(a0, a_name):
+        outer = lax.axis_size(a_name)
+        known = jnp.stack(outer * [a0], axis=0)
+        n_now = lax.all_to_all(known, axis_name=a_name, concat_axis=0, split_axis=0)
+        arr_out = jnp.concatenate(n_now, axis=0)
+        return arr_out
+
     own_rows = hidden_in.astype(jnp.float32)
     raw_rows = lax.all_gather(hidden_in, "head", axis=0, tiled=True)
     normed = root_mean_scale(raw_rows.astype(jnp.float32), pre_gain).astype(jnp.bfloat16)
@@ -60,7 +68,7 @@
         return jnp.dot(normed, weight_piece, preferred_element_type=jnp.float32)
 
     query_raw = add_rows(lax.all_gather(w_query, "ctx", axis=0, tiled=True))
-    key_unnormed = add_rows(lax.all_gather(w_key, "ctx", axis=0, tiled=True))
+    key_unnormed = add_rows(stops_all_get(w_key, a_name="ctx"))
     value_unnormed = add_rows(lax.all_gather(value_weight, "ctx", axis=0, tiled=True))
     local_heads = w_query.shape[1] // HEAD_SIZE
     local_groups = w_key.shape[1] // HEAD_SIZE

time: 401 us -> 364 us (0.908)
  waiting for transfers between devices: 312 us -> 266 us
  starting transfers between devices: 3.56 us -> 10.6 us
    all_gather x1 -> x0, waiting for transfers between devices: 39.5 us -> none  [body(): key_unnormed = add_rows(lax.all_gather(w_key, 'ctx', axis=0, tiled=True))]
    all_gather x1, waiting for transfers between devices: 41.1 us -> 31.9 us  [body(): lax.all_gather(value_weight, 'ctx', axis=0, tiled=True)]
    all_to_all x0 -> x1, starting transfers between devices: none -> 7.04 us  [stops_all_get(): n_now = lax.all_to_all(known, axis_name=a_name, concat_axis=0, split_axis=0)]
  transfers between devices with their start and end apart: 7 -> 7, of which waited for: 6 -> 5; matrix products, arithmetic and copies ran while one was open for 15% -> 17% of each run, Pallas kernels for 0% -> 0%
where the time goes in v1:
time: 364 us; the launch traced here: 363 us
  waiting for transfers between devices  266 us (73%)
  matrix products  40 us (11%)
  other arithmetic  29 us (8%)
  between operations  13.4 us (4%)
  starting transfers between devices  10.6 us (3%)
  local copies, waits for them, and re-layouts  4.56 us (1%)
    reduce_scatter x1, waiting for transfers between devices, body(): lax.psum_scatter(lax.optimization_barrier(partial_value).astype(jnp.float...  78.9 us
    all_gather x1, waiting for transfers between devices, body(): raw_rows = lax.all_gather(hidden_in, 'head', axis=0, tiled=True)  61.8 us
    all_gather x1, waiting for transfers between devices, body(): query_raw = add_rows(lax.all_gather(w_query, 'ctx', axis=0, tiled=True))  52.2 us
    all_gather x1, waiting for transfers between devices, body(): out_weight = lax.all_gather(w_output, 'ctx', axis=0, tiled=True)  38.5 us
    all_gather x1, waiting for transfers between devices, body(): lax.all_gather(value_weight, 'ctx', axis=0, tiled=True)  31.9 us
    dot_general x3, matrix products, add_rows(): return jnp.dot(normed, weight_piece, preferred_element_type=jnp.float32)  25.6 us
    reduce_sum x2, other arithmetic, root_mean_scale(): mean_sq = jnp.mean(values * values, axis=-1, keepdims=True)  7.81 us
    dot_general x1, matrix products, body(): jnp.dot(attended, out_weight, preferred_element_type=jnp.float32)  7.65 us
  transfers between devices with their start and end apart: 7, of which 5 were waited for; matrix products, arithmetic and copies ran while one was open for 17% of the time, Pallas kernels for 0%

profile of v1, /device:TPU:0, one launch (start us, length us, event | category | flops | bytes accessed | tf_op | source)
XLA Modules:
  0.0 363.4 jit_solution(10609285395235612970)
XLA Ops:
  6.5 0.0 all-gather.5.cloned.1.call-start
  6.5 0.7 all-gather.5.cloned.1.call-update
  7.3 0.0 all-gather.7.cloned.1.call-start
  7.3 0.7 all-gather.7.cloned.1.call-update
  8.0 0.0 all-gather.9.cloned.1.call-start
  8.1 0.7 all-gather.9.cloned.1.call-update
  8.7 2.2 stack.6
  10.9 7.0 %all-to-all-start = ((bf16[8,672,128]{2,1,0:T(8,128)(2,1)}), bf16[8,672,128]{2,1,0:T(8,128)(2,1)}, u32[]{:S(2)}, u32[]{:S(2)}) async-start(bf16[8,672,128]{2,1,0:T(8,128)(2,1)} %stack.6), calls=%async_computation | async-start | bytes 2752512 | tf_op jit(solution)/shard_map/all_to_all | solution.py:58
  18.0 0.0 all-gather.11.cloned.1.call-start
  18.0 0.5 all-gather.11.cloned.1.call-update
  18.6 0.0 reduce-scatter.2.cloned.1.call-start
  18.7 3.1 multiply_cosine_fusion
  21.8 0.0 copy-start.6
  21.8 1.8 and_and_fusion.1
  23.6 1.9 and_and_fusion
  25.5 61.8 %all-gather.5.cloned.1.call-done = bf16[1024,5376]{1,0:T(8,128)(2,1)} async-done(((bf16[64,5376]{1,0:T(8,128)(2,1)}), bf16[1024,5376]{1,0:T(8,128)(2,1)}) %all-gather.5.cloned.1.call-update) | async-done | bytes 11010064 | tf_op jit(solution)/shard_map/all_gather | solution.py:63
  87.2 0.0 copy-start
  87.2 6.5 %fusion = f32[1024]{0:T(1024)S(1)} fusion(bf16[1024,5376]{1,0:T(8,128)(2,1)} %all-gather.5.cloned.1.call-done), kind=kLoop, calls=%fused_computation.2 | loop fusion | flops 16514048 | bytes 11014144 | tf_op jit(solution)/shard_map/reduce_sum | solution.py:21
  93.7 0.0 copy-done.6
  93.7 0.8 copy-done
  94.5 6.0 %fusion.2 = bf16[1024,5376]{1,0:T(8,128)(2,1)} fusion(bf16[1024,5376]{1,0:T(8,128)(2,1)S(1)} %copy-done, f32[5376]{0:T(1024)S(1)} %copy-done.6, f32[1024]{0:T(1024)S(1)} %add_rsqrt_fusion.2), kind=kLoop, calls=%fused_computation.4 | loop fusion | flops 22020096 | bytes 22045696 | tf_op jit(solution)/shard_map/convert_element_type | solution.py:64
  100.5 0.0 all-to-all-done
  100.5 0.0 copy-start.8
  100.5 8.4 %multiply_reduce_fusion.1 = (f32[1024]{0:T(1024)S(1)}, f32[1024,128]{0,1:T(8,128)S(1)}) fusion(bf16[1024,5376]{1,0:T(8,128)(2,1)} %fusion.2, bf16[5376,128]{1,0:T(8,128)(2,1)} %bitcast), kind=kOutput, calls=%fused_computation.46 | convolution fusion | flops 1409547264 | bytes 12914688 | tf_op jit(solution)/shard_map/dot_general | solution.py:68
  108.9 0.0 copy-done.8
  108.9 0.1 multiply_bitcast_fusion
  109.0 1.2 fusion.39
  110.2 31.9 %all-gather.7.cloned.1.call-done = bf16[5376,128]{1,0:T(8,128)(2,1)} async-done(((bf16[672,128]{1,0:T(8,128)(2,1)}), bf16[5376,128]{1,0:T(8,128)(2,1)}) %all-gather.7.cloned.1.call-update) | async-done | bytes 1376272 | tf_op jit(solution)/shard_map/all_gather | solution.py:72
  142.1 8.2 %fusion.21 = bf16[1,1024,128]{1,2,0:T(8,128)(2,1)S(1)} fusion(bf16[1024,5376]{1,0:T(8,128)(2,1)} %fusion.2, bf16[5376,128]{1,0:T(8,128)(2,1)} %all-gather.7.cloned.1.call-done), kind=kOutput, calls=%fused_computation.31 | convolution fusion | flops 1409417216 | bytes 12648448 | tf_op jit(solution)/shard_map/dot_general | solution.py:68
  150.3 0.0 copy-start.9
  150.4 0.0 copy-start.4
  150.4 0.0 copy-start.5
  150.4 3.4 collective-permute-start
  153.7 52.2 %all-gather.9.cloned.1.call-done = bf16[5376,256]{1,0:T(8,128)(2,1)} async-done(((bf16[672,256]{1,0:T(8,128)(2,1)}), bf16[5376,256]{1,0:T(8,128)(2,1)}) %all-gather.9.cloned.1.call-update) | async-done | bytes 2752528 | tf_op jit(solution)/shard_map/all_gather | solution.py:70
  206.0 9.0 %multiply_reduce_fusion = (f32[1024,2]{0,1:T(2,128)S(1)}, f32[1024,256]{0,1:T(8,128)}) fusion(bf16[1024,5376]{1,0:T(8,128)(2,1)} %fusion.2, bf16[5376,256]{1,0:T(8,128)(2,1)} %all-gather.9.cloned.1.call-done), kind=kOutput, calls=%fused_computation.38 | convolution fusion | flops 2819094528 | bytes 14819328 | tf_op jit(solution)/shard_map/dot_general | solution.py:68
  214.9 1.6 copy.11
  216.5 0.0 copy-start.1
  216.5 0.0 copy-done.9
  216.6 0.3 multiply_multiply_fusion
  216.9 0.0 copy-done.4
  216.9 0.0 copy-done.5
  216.9 0.5 multiply_subtract_fusion
  217.4 0.0 copy-start.2
  217.4 0.3 fusion.22
  217.8 0.0 collective-permute-done
  217.8 1.1 maximum_maximum_fusion
  218.9 0.0 copy-done.1
  218.9 1.3 fusion.3
  220.2 0.0 copy-done.2
  220.2 1.3 fusion.4
  221.5 1.2 fusion.5
  222.8 1.2 fusion.6
  224.0 2.0 fusion.15
  226.0 2.2 fusion.18
  228.2 38.5 %all-gather.11.cloned.1.call-done = bf16[256,5376]{1,0:T(8,128)(2,1)} async-done(((bf16[32,5376]{1,0:T(8,128)(2,1)}), bf16[256,5376]{1,0:T(8,128)(2,1)}) %all-gather.11.cloned.1.call-update) | async-done | bytes 2752528 | tf_op jit(solution)/shard_map/all_gather | solution.py:130
  266.7 7.6 %convolution_convert_fusion = bf16[1024,5376]{1,0:T(8,128)(2,1)} fusion(bf16[256,5376]{1,0:T(8,128)(2,1)} %all-gather.11.cloned.1.call-done, bf16[512,256]{0,1:T(8,128)(2,1)S(1)} %bitcast.96, bf16[512,256]{0,1:T(8,128)(2,1)S(1)} %bitcast.95), kind=kOutput, calls=%fused_computation.5 | convolution fusion | flops 2825125888 | bytes 14286848 | tf_op jit(solution)/shard_map/dot_general | solution.py:131
  274.4 0.0 copy-start.3
  274.4 0.0 copy-start.7
  274.4 0.0 reduce-scatter.2.cloned.1.call-update
  274.4 78.9 %reduce-scatter.2.cloned.1.call-done = bf16[64,5376]{1,0:T(8,128)(2,1)} async-done(((bf16[1024,5376]{1,0:T(8,128)(2,1)}), bf16[64,5376]{1,0:T(8,128)(2,1)}) %reduce-scatter.2.cloned.1.call-update) | async-done | bytes 688144 | tf_op jit(solution)/shard_map/reduce_scatter | solution.py:134
  353.3 1.3 fusion.11
  354.6 0.0 copy-done.3
  354.6 0.0 copy-done.7
  354.6 2.3 fusion.14
  (12 shorter events, 0.1 us)
Async XLA Ops:
  6.5 80.7 %all-gather.5.cloned.1.call-start = ((), (), s32[]{:S(2)}) async-start(), calls=%async_computation.2 | async-start | bytes 11698176 | tf_op jit(solution)/shard_map/all_gather | solution.py:63
  7.3 134.8 %all-gather.7.cloned.1.call-start = ((), (), s32[]{:S(2)}) async-start(), calls=%async_computation.3 | async-start | bytes 1548288 | tf_op jit(solution)/shard_map/all_gather | solution.py:72
  8.0 198.0 %all-gather.9.cloned.1.call-start = ((), (), s32[]{:S(2)}) async-start(), calls=%async_computation.4 | async-start | bytes 3096576 | tf_op jit(solution)/shard_map/all_gather | solution.py:70
  10.9 89.5 %all-to-all-start = ((bf16[8,672,128]{2,1,0:T(8,128)(2,1)}), bf16[8,672,128]{2,1,0:T(8,128)(2,1)}, u32[]{:S(2)}, u32[]{:S(2)}) async-start(bf16[8,672,128]{2,1,0:T(8,128)(2,1)} %stack.6), calls=%async_computation | async-start | bytes 2752512 | tf_op jit(solution)/shard_map/all_to_all | solution.py:58
  18.0 248.7 %all-gather.11.cloned.1.call-start = ((), (), s32[]{:S(2)}) async-start(), calls=%async_computation.5 | async-start | bytes 3096576 | tf_op jit(solution)/shard_map/all_gather | solution.py:130
  18.6 334.7 %reduce-scatter.2.cloned.1.call-start = ((), (), s32[]{:S(2)}) async-start(), calls=%async_computation.6 | async-start | bytes 11698176 | tf_op jit(solution)/shard_map/reduce_scatter | solution.py:134
  21.8 72.0 %copy-start.6 = (f32[5376]{0:T(1024)S(1)}, f32[5376]{0:T(1024)}, u32[]{:S(2)}) copy-start(f32[5376]{0:T(1024)} %param.10) | copy-start | bytes 64516
  87.2 7.3 %copy-start = (bf16[1024,5376]{1,0:T(8,128)(2,1)S(1)}, bf16[1024,5376]{1,0:T(8,128)(2,1)}, u32[]{:S(2)}) copy-start(bf16[1024,5376]{1,0:T(8,128)(2,1)} %all-gather.5.cloned.1.call-done) | copy-start | bytes 33030148
  100.5 8.4 %copy-start.8 = (f32[128]{0:T(128)S(1)}, f32[128]{0:T(128)}, u32[]{:S(2)}) copy-start(f32[128]{0:T(128)} %param.15) | copy-start | bytes 1540
  150.3 66.2 %copy-start.9 = (f32[128]{0:T(128)S(1)}, f32[128]{0:T(128)}, u32[]{:S(2)}) copy-start(f32[128]{0:T(128)} %param.14) | copy-start | bytes 1540
  150.4 66.5 %copy-start.4 = (f32[1024,64]{1,0:T(8,128)S(1)}, f32[1024,64]{1,0:T(8,128)}, u32[]{:S(2)}) copy-start(f32[1024,64]{1,0:T(8,128)} %get-tuple-element.9) | copy-start | bytes 786436
  150.4 66.5 %copy-start.5 = (f32[1024,64]{1,0:T(8,128)S(1)}, f32[1024,64]{1,0:T(8,128)}, u32[]{:S(2)}) copy-start(f32[1024,64]{1,0:T(8,128)} %get-tuple-element.10) | copy-start | bytes 786436
  150.4 67.4 %collective-permute-start = (bf16[2,1024,128]{1,2,0:T(8,128)(2,1)S(1)}, bf16[2,1024,128]{1,2,0:T(8,128)(2,1)}, u32[]{:S(2)}, u32[]{:S(2)}) collective-permute-start(bf16[2,1024,128]{1,2,0:T(8,128)(2,1)S(1)} %pad_maximum_fusion), channel_id=1, source_target_pairs={{0,16},{16,32},{32,48},{48,64},{64,80},{80,96},{96,112},{1,17},{17... | collective-permute-start | bytes 1572872 | tf_op jit(solution)/shard_map/ppermute | solution.py:17
  216.5 2.4 copy-start.1
  217.4 2.8 copy-start.2
  274.4 80.3 %copy-start.3 = (bf16[64,5376]{1,0:T(8,128)(2,1)S(1)}, bf16[64,5376]{1,0:T(8,128)(2,1)}, u32[]{:S(2)}) copy-start(bf16[64,5376]{1,0:T(8,128)(2,1)} %param.9) | copy-start | bytes 2064388
  274.4 80.3 %copy-start.7 = (f32[5376]{0:T(1024)S(1)}, f32[5376]{0:T(1024)}, u32[]{:S(2)}) copy-start(f32[5376]{0:T(1024)} %param.17) | copy-start | bytes 64516
Sparse Core Ops, SparseCore 0:
  9.0 78.1 all-gather.4
  89.6 52.4 all-gather.6
  144.4 61.5 all-gather.8
  208.1 58.5 all-gather.10
  274.5 78.7 reduce-scatter.1
